TPU v7x, 512 devices: a whole 4x4x16 slice. The times are simulated.
512 devices in a mesh: dp: 8 (over x, y_hi), expert: 64 (over y_lo, z, core).
Axes of the slice: x: 4, y: 4 (y_hi: 2, y_lo: 2; y = y_hi * 2 + y_lo), z: 16, core: 2. Of those that a mesh axis runs over, the one named last changes fastest.
Arguments:
- tokens: bfloat16 [65536, 2048], P(('dp', 'expert')), may hold values from -6 to 6
- out_grad: bfloat16 [65536, 2048], P(('dp', 'expert')), may hold values from -6 to 6
- combine: float32 [65536, 2], P(('dp', 'expert')), may hold values from 0.1 to 1
- expert_ids: int32 [65536, 2], P(('dp', 'expert')), may hold values from 0 to 63, all different within a row; in each aligned block of 128 rows (0 to 127, 128 to 255, ...) at most 5 rows name the same one
- gate_weight: bfloat16 [64, 2048, 768], P('expert', 'dp'), may hold values from -0.125 to 0.125
- up_weight: bfloat16 [64, 2048, 768], P('expert', 'dp'), may hold values from -0.125 to 0.125
- down_weight: bfloat16 [64, 2048, 768], P('expert', 'dp'), may hold values from -0.21875 to 0.21875
Outputs:
- token_grad: bfloat16 [65536, 2048], P(('dp', 'expert'))
- down_grad: bfloat16 [64, 2048, 768], P('expert', 'dp')
Inputs may be any that keep to these rules, and one draw needn't show every extreme that they name: `expert_ids`: each row names 2 different experts. Among the 128 rows of one device no expert is named more than 5 times, a bound that some block reaches.
All inputs are finite; a program needn't handle non-finite values.
Results may differ from a plain program's by a relative error of at most 0.012.
Values may be sent and summed in bfloat16 or wider, within the bound.
No kernel may reach another device: no remote copies, remote signals or barrier semaphores. Data moves between devices by JAX's collectives and lax.ppermute only.
A program may use at most 64 MiB of HBM per device.

v0:
```python
import jax
import jax.numpy as jnp
from jax import lax
from jax.sharding import PartitionSpec as P

TOP = 2


def forward_portion(rows_in, w_gate, w_up):
    gate_pre = jnp.dot(rows_in, w_gate, preferred_element_type=jnp.float32)
    up_pre = jnp.dot(rows_in, w_up, preferred_element_type=jnp.float32)
    sigmoid_gate = jax.nn.sigmoid(gate_pre)
    silu_gate = gate_pre * sigmoid_gate
    hidden = (silu_gate * up_pre).astype(jnp.bfloat16)
    return (gate_pre, up_pre, sigmoid_gate, silu_gate, hidden)


def body(tokens, out_grad, combine, expert_ids, gate_weight, up_weight, down_weight):
    token_rows = tokens.shape[0]
    embedding_width = tokens.shape[1]
    expert_count = lax.axis_size("expert")
    capacity = token_rows * TOP * 5 // (4 * expert_count)
    positions = expert_count * capacity
    flattened_identifiers = expert_ids.reshape(-1)
    onehot = (
        flattened_identifiers[:, None] == jnp.arange(expert_count, dtype=jnp.int32)[None, :]
    ).astype(jnp.int32)
    earlier = jnp.cumsum(onehot, axis=0) - onehot
    slot_index = jnp.sum(earlier * onehot, axis=1)
    target = flattened_identifiers * capacity + slot_index
    matches = target[None, :] == jnp.arange(positions, dtype=jnp.int32)[:, None]
    picker = jnp.sum(
        matches.reshape(positions, token_rows, TOP).astype(jnp.float32), axis=2
    ).astype(jnp.bfloat16)
    slot_weight = jnp.sum(
        jnp.where(matches, combine.reshape(-1)[None, :], jnp.float32(0.0)), axis=1
    )
    row_send = jnp.dot(picker, tokens, preferred_element_type=jnp.float32).astype(jnp.bfloat16)
    row_send = row_send.reshape(expert_count, capacity, embedding_width)
    picked_grad = jnp.dot(picker, out_grad, preferred_element_type=jnp.float32)
    grad_send = (slot_weight[:, None] * picked_grad).astype(jnp.bfloat16)
    grad_send = grad_send.reshape(expert_count, capacity, embedding_width)
    gathered = (
        lax.all_gather(gate_weight, "dp", axis=1, tiled=True),
        lax.all_gather(up_weight, "dp", axis=1, tiled=True),
        lax.all_gather(down_weight, "dp", axis=1, tiled=True),
    )
    w_gate = gathered[0][0]
    w_up = gathered[1][0]
    w_down = gathered[2][0]
    rows_in, grads_in = (
        lax.all_to_all(row_send, "expert", split_axis=0, concat_axis=0, tiled=True),
        lax.all_to_all(grad_send, "expert", split_axis=0, concat_axis=0, tiled=True),
    )
    rows_in = rows_in.reshape(positions, embedding_width)
    grads_in = grads_in.reshape(positions, embedding_width)
    gate_pre, up_pre, sigmoid_gate, silu_gate, hidden = forward_portion(rows_in, w_gate, w_up)
    hidden_grad = jnp.dot(grads_in, w_down, preferred_element_type=jnp.float32)
    gate_grad = (
        hidden_grad * up_pre * sigmoid_gate * (1.0 + gate_pre * (1.0 - sigmoid_gate))
    ).astype(jnp.bfloat16)
    up_grad = (hidden_grad * silu_gate).astype(jnp.bfloat16)
    contract_hidden = (((1,), (1,)), ((), ()))
    row_grad = (
        lax.dot_general(gate_grad, w_gate, contract_hidden, preferred_element_type=jnp.float32)
        + lax.dot_general(up_grad, w_up, contract_hidden, preferred_element_type=jnp.float32)
    ).astype(jnp.bfloat16)
    back_rows = lax.all_to_all(
        row_grad.reshape(expert_count, capacity, embedding_width),
        "expert",
        split_axis=0,
        concat_axis=0,
        tiled=True,
    )
    token_grad = lax.dot_general(
        picker,
        back_rows.reshape(positions, embedding_width),
        (((0,), (0,)), ((), ())),
        preferred_element_type=jnp.float32,
    ).astype(jnp.bfloat16)
    down_grad = lax.psum_scatter(
        lax.dot_general(
            grads_in, hidden, (((0,), (0,)), ((), ())), preferred_element_type=jnp.float32
        ).astype(jnp.bfloat16),
        "dp",
        scatter_dimension=0,
        tiled=True,
    )
    return (token_grad, down_grad[None])


def solution(mesh):
    placed = (
        P(("dp", "expert"), None),
        P(("dp", "expert"), None),
        P(("dp", "expert"), None),
        P(("dp", "expert"), None),
        P("expert", "dp", None),
        P("expert", "dp", None),
        P("expert", "dp", None),
    )
    return jax.shard_map(
        body,
        mesh=mesh,
        in_specs=placed,
        out_specs=(P(("dp", "expert"), None), P("expert", "dp", None)),
        check_vma=False,
    )
```

profile of v0, /device:TPU:33, one launch (start us, length us, event | category | flops | bytes accessed | tf_op | source)
XLA Modules:
  0.0 401.3 jit_solution(16385939312701261271)
XLA Ops:
  7.2 0.0 copy-start
  7.2 0.0 all-gather.8.cloned.1.call-start
  7.2 0.7 all-gather.8.cloned.1.call-update
  7.9 0.8 copy.23
  8.7 0.1 eq.49
  8.8 0.1 eq.45
  9.0 0.6 reduce-window.6
  9.6 0.2 slice_reduce_fusion
  9.8 0.1 fusion.23
  9.9 0.1 reduce_sum.30
  10.1 0.1 copy.26
  10.2 0.8 copy.27
  11.0 0.1 broadcast_in_dim.21
  11.1 0.7 multiply_add_fusion.1
  11.9 0.1 select_reduce_fusion
  12.0 0.0 copy-done
  12.0 0.5 fusion.16
  12.5 1.6 reshape.61
  14.1 0.0 copy-start.2
  14.1 17.2 %all-to-all-start = ((bf16[64,5,2048]{2,1,0:T(8,128)(2,1)}), bf16[64,5,2048]{2,1,0:T(8,128)(2,1)S(1)}, u32[]{:S(2)}, u32[]{:S(2)}) async-start(bf16[64,5,2048]{2,1,0:T(8,128)(2,1)} %reshape.61), calls=%async_computation | async-start | bytes 4194304 | tf_op jit(solution)/shard_map/all_to_all | solution.py:53
  31.4 0.0 all-gather.6.cloned.1.call-start
  31.4 0.7 all-gather.6.cloned.1.call-update
  32.1 0.0 copy-done.2
  32.1 1.6 convolution_convert_fusion.1
  33.7 3.4 reshape.63
  37.1 92.3 %all-to-all-done = bf16[64,5,2048]{2,1,0:T(8,128)(2,1)S(1)} async-done(((bf16[64,5,2048]{2,1,0:T(8,128)(2,1)}), bf16[64,5,2048]{2,1,0:T(8,128)(2,1)S(1)}, u32[]{:S(2)}, u32[]{:S(2)}) %all-to-all-start) | async-done | bytes 1310752 | tf_op jit(solution)/shard_map/all_to_all | solution.py:53
  129.4 7.1 %all-to-all-start.1 = ((bf16[64,5,2048]{2,1,0:T(8,128)(2,1)}), bf16[64,5,2048]{2,1,0:T(8,128)(2,1)}, u32[]{:S(2)}, u32[]{:S(2)}) async-start(bf16[64,5,2048]{2,1,0:T(8,128)(2,1)} %reshape.63), calls=%async_computation.1 | async-start | bytes 4194304 | tf_op jit(solution)/shard_map/all_to_all | solution.py:52
  136.6 0.0 all-gather.4.cloned.1.call-start
  136.6 0.7 all-gather.4.cloned.1.call-update
  137.3 0.2 reduce-scatter.2.cloned.1.call-start
  137.5 1.4 reshape.62
  139.0 95.6 %all-to-all-done.1 = bf16[64,5,2048]{2,1,0:T(8,128)(2,1)} async-done(((bf16[64,5,2048]{2,1,0:T(8,128)(2,1)}), bf16[64,5,2048]{2,1,0:T(8,128)(2,1)}, u32[]{:S(2)}, u32[]{:S(2)}) %all-to-all-start.1) | async-done | bytes 1310752 | tf_op jit(solution)/shard_map/all_to_all | solution.py:52
  234.5 2.6 reshape.64
  237.1 0.0 all-gather.8.cloned.1.call-done
  237.1 4.0 %fusion.2 = f32[320,768]{1,0:T(8,128)} fusion(bf16[320,2048]{1,0:T(8,128)(2,1)S(1)} %reshape.64, bf16[1,2048,768]{2,1,0:T(8,128)(2,1)} %all-gather.8.cloned.1.call-done), kind=kOutput, calls=%fused_computation.3 | convolution fusion | flops 1006632960 | bytes 5439488 | tf_op jit(solution)/shard_map/dot_general | solution.py:10
  241.2 0.0 copy-start.1
  241.2 0.0 all-gather.6.cloned.1.call-done
  241.2 0.0 copy-start.5
  241.2 3.2 fusion.6
  244.4 0.0 copy-start.7
  244.4 1.0 copy-done.7
  245.4 0.0 copy-done.1
  245.4 0.0 copy-done.5
  245.4 3.7 convolution_convert_fusion
  249.0 0.0 reduce-scatter.2.cloned.1.call-update
  249.1 0.0 copy-start.6
  249.1 20.1 %all-gather.4.cloned.1.call-done = bf16[1,2048,768]{2,1,0:T(8,128)(2,1)} async-done(((bf16[1,256,768]{2,1,0:T(8,128)(2,1)}), bf16[1,2048,768]{2,1,0:T(8,128)(2,1)}) %all-gather.4.cloned.1.call-update) | async-done | bytes 3145744 | tf_op jit(solution)/shard_map/all_gather | solution.py:46
  269.2 0.0 copy-start.3
  269.2 0.0 copy-start.8
  269.2 3.2 fusion.8
  272.4 0.0 copy-done.6
  272.5 0.0 copy-done.3
  272.5 0.0 copy-done.8
  272.5 0.0 copy-start.4
  272.5 1.3 fusion
  273.8 0.5 copy-done.4
  274.4 2.3 fusion.13
  276.7 2.4 reshape.65
  279.0 111.9 %all_to_all.15 = bf16[64,5,2048]{2,1,0:T(8,128)(2,1)} all-to-all(bf16[64,5,2048]{2,1,0:T(8,128)(2,1)S(1)} %reshape.65), channel_id=1, replica_groups=mesh['dp'=8,'expert'=64] {'expert'}, dimensions={0} | all-to-all | bytes 2621440 | tf_op jit(solution)/shard_map/all_to_all | solution.py:68
  391.0 2.6 reshape.66
  393.5 1.3 convolution_convert_fusion.2
  394.8 0.0 reduce-scatter.2.cloned.1.call-done
  (5 shorter events, 0.1 us)
Async XLA Ops:
  7.2 4.8 %copy-start = (bf16[128,2048]{1,0:T(8,128)(2,1)S(1)}, bf16[128,2048]{1,0:T(8,128)(2,1)}, u32[]{:S(2)}) copy-start(bf16[128,2048]{1,0:T(8,128)(2,1)} %param.8) | copy-start | bytes 1572868
  7.2 229.9 %all-gather.8.cloned.1.call-start = ((), (), s32[]{:S(2)}) async-start(), calls=%async_computation.6 | async-start | bytes 3538944 | tf_op jit(solution)/shard_map/all_gather | solution.py:44
  14.1 18.0 %copy-start.2 = (bf16[128,2048]{1,0:T(8,128)(2,1)S(1)}, bf16[128,2048]{1,0:T(8,128)(2,1)}, u32[]{:S(2)}) copy-start(bf16[128,2048]{1,0:T(8,128)(2,1)} %param.7) | copy-start | bytes 1572868
  14.1 115.3 %all-to-all-start = ((bf16[64,5,2048]{2,1,0:T(8,128)(2,1)}), bf16[64,5,2048]{2,1,0:T(8,128)(2,1)S(1)}, u32[]{:S(2)}, u32[]{:S(2)}) async-start(bf16[64,5,2048]{2,1,0:T(8,128)(2,1)} %reshape.61), calls=%async_computation | async-start | bytes 4194304 | tf_op jit(solution)/shard_map/all_to_all | solution.py:53
  31.4 209.8 %all-gather.6.cloned.1.call-start = ((), (), s32[]{:S(2)}) async-start(), calls=%async_computation.5 | async-start | bytes 3538944 | tf_op jit(solution)/shard_map/all_gather | solution.py:45
  129.4 105.1 %all-to-all-start.1 = ((bf16[64,5,2048]{2,1,0:T(8,128)(2,1)}), bf16[64,5,2048]{2,1,0:T(8,128)(2,1)}, u32[]{:S(2)}, u32[]{:S(2)}) async-start(bf16[64,5,2048]{2,1,0:T(8,128)(2,1)} %reshape.63), calls=%async_computation.1 | async-start | bytes 4194304 | tf_op jit(solution)/shard_map/all_to_all | solution.py:52
  136.6 132.7 %all-gather.4.cloned.1.call-start = ((), (), s32[]{:S(2)}) async-start(), calls=%async_computation.4 | async-start | bytes 3538944 | tf_op jit(solution)/shard_map/all_gather | solution.py:46
  137.3 257.5 %reduce-scatter.2.cloned.1.call-start = ((), (), s32[]{:S(2)}) async-start(), calls=%async_computation.7 | async-start | bytes 3538944 | tf_op jit(solution)/shard_map/reduce_scatter | solution.py:81
  241.2 4.2 %copy-start.1 = (bf16[320,2048]{1,0:T(8,128)(2,1)S(1)}, bf16[320,2048]{1,0:T(8,128)(2,1)}, u32[]{:S(2)}) copy-start(bf16[320,2048]{1,0:T(8,128)(2,1)} %reshape.62) | copy-start | bytes 3932164
  241.2 4.2 %copy-start.5 = (f32[320,768]{1,0:T(8,128)S(1)}, f32[320,768]{1,0:T(8,128)}, u32[]{:S(2)}) copy-start(f32[320,768]{1,0:T(8,128)} %fusion.2) | copy-start | bytes 2949124
  244.4 1.0 copy-start.7
  249.1 23.4 %copy-start.6 = (f32[320,768]{1,0:T(8,128)S(1)}, f32[320,768]{1,0:T(8,128)}, u32[]{:S(2)}) copy-start(f32[320,768]{1,0:T(8,128)} %fusion.2) | copy-start | bytes 2949124
  269.2 3.2 copy-start.3
  269.2 3.2 copy-start.8
  272.5 1.9 copy-start.4
Sparse Core Ops, SparseCore 0:
  11.2 88.6 all-gather.7
  103.0 82.7 all-gather.5
  189.0 80.1 all-gather.3
  274.4 99.4 reduce-scatter.1
where the time goes:
time: 402 us; the launch traced here: 401 us
  waiting for transfers between devices  210 us (52%)
  blocking collectives  112 us (28%)
  starting transfers between devices  24.7 us (6%)
  matrix products  21.1 us (5%)
  local copies, waits for them, and re-layouts  17.9 us (4%)
  between operations  14 us (3%)
    all_to_all x1, blocking collectives, body(): lax.all_to_all(row_grad.reshape(expert_count, capacity, embedding_width),...  112 us
    all_to_all x1, waiting for transfers between devices, body(): lax.all_to_all(row_send, 'expert', split_axis=0, concat_axis=0, tiled=True)  95.6 us
    all_to_all x1, waiting for transfers between devices, body(): lax.all_to_all(grad_send, 'expert', split_axis=0, concat_axis=0, tiled=True)  92.3 us
    all_gather x1, waiting for transfers between devices, body(): lax.all_gather(down_weight, 'dp', axis=1, tiled=True)  20.1 us
    all_to_all x1, starting transfers between devices, body(): lax.all_to_all(grad_send, 'expert', split_axis=0, concat_axis=0, tiled=True)  17.2 us
  transfers between devices with their start and end apart: 6, of which 3 were waited for; matrix products, arithmetic and copies ran while one was open for 10% of the time, Pallas kernels for 0%

commit v1 on v0

--- a/solution.py
+++ b/solution.py
@@ -43,7 +43,9 @@
     gathered = (
         lax.all_gather(gate_weight, "dp", axis=1, tiled=True),
         lax.all_gather(up_weight, "dp", axis=1, tiled=True),
-        lax.all_gather(down_weight, "dp", axis=1, tiled=True),
+        jnp.concatenate(
+            lax.all_to_all(jnp.stack([down_weight] * lax.axis_size("dp")), "dp", 0, 0), axis=1
+        ),
     )
     w_gate = gathered[0][0]
     w_up = gathered[1][0]

time: 402 us -> 429 us (1.067)
  waiting for transfers between devices: 210 us -> 232 us
  starting transfers between devices: 24.7 us -> 30.9 us
  blocking collectives: 112 us -> 106 us
    all_to_all x0 -> x1, waiting for transfers between devices: none -> 40.8 us  [body(): lax.all_to_all(jnp.stack([down_weight] * lax.axis_size('dp')), 'dp', 0, 0)]
    all_gather x1 -> x0, waiting for transfers between devices: 20.1 us -> none  [body(): lax.all_gather(down_weight, 'dp', axis=1, tiled=True)]
    all_to_all x1, blocking collectives: 112 us -> 106 us  [body(): lax.all_to_all(row_grad.reshape(expert_count, capacity, embedding_width),...]
    all_to_all x0 -> x1, starting transfers between devices: none -> 6.36 us  [body(): lax.all_to_all(jnp.stack([down_weight] * lax.axis_size('dp')), 'dp', 0, 0)]
  transfers between devices with their start and end apart: 6 -> 6, of which waited for: 3 -> 3; matrix products, arithmetic and copies ran while one was open for 10% -> 7% of each run, Pallas kernels for 0% -> 0%
where the time goes in v1:
time: 429 us
  waiting for transfers between devices  232 us (54%)
  blocking collectives  106 us (25%)
  starting transfers between devices  30.9 us (7%)
  matrix products  24.1 us (6%)
  local copies, waits for them, and re-layouts  20.8 us (5%)
  between operations  13.9 us (3%)
    all_to_all x1, blocking collectives, body(): lax.all_to_all(row_grad.reshape(expert_count, capacity, embedding_width),...  106 us
    all_to_all x1, waiting for transfers between devices, body(): lax.all_to_all(row_send, 'expert', split_axis=0, concat_axis=0, tiled=True)  97.2 us
    all_to_all x1, waiting for transfers between devices, body(): lax.all_to_all(grad_send, 'expert', split_axis=0, concat_axis=0, tiled=True)  92.3 us
    all_to_all x1, waiting for transfers between devices, body(): lax.all_to_all(jnp.stack([down_weight] * lax.axis_size('dp')), 'dp', 0, 0)  40.8 us
    all_to_all x1, starting transfers between devices, body(): lax.all_to_all(grad_send, 'expert', split_axis=0, concat_axis=0, tiled=True)  17.2 us
  transfers between devices with their start and end apart: 6, of which 3 were waited for; matrix products, arithmetic and copies ran while one was open for 7% of the time, Pallas kernels for 0%

profile of v1, /device:TPU:33, one launch (start us, length us, event | category | flops | bytes accessed | tf_op | source)
XLA Modules:
  0.0 428.6 jit_solution(10852453414962049748)
XLA Ops:
  7.2 0.0 copy-start
  7.2 0.8 copy.23
  8.0 0.1 eq.49
  8.2 0.1 eq.45
  8.3 0.6 reduce-window.6
  8.9 0.2 slice_reduce_fusion
  9.2 0.1 fusion.21
  9.3 0.1 reduce_sum.30
  9.4 0.1 copy.26
  9.5 0.7 multiply_add_fusion.1
  10.2 0.8 copy.27
  11.0 0.1 broadcast_in_dim.21
  11.2 0.2 select_reduce_fusion
  11.3 0.0 copy-done
  11.3 0.5 fusion.14
  11.8 1.6 reshape.64
  13.5 0.0 copy-start.2
  13.5 17.2 %all-to-all-start = ((bf16[64,5,2048]{2,1,0:T(8,128)(2,1)}), bf16[64,5,2048]{2,1,0:T(8,128)(2,1)S(1)}, u32[]{:S(2)}, u32[]{:S(2)}) async-start(bf16[64,5,2048]{2,1,0:T(8,128)(2,1)} %reshape.64), calls=%async_computation | async-start | bytes 4194304 | tf_op jit(solution)/shard_map/all_to_all | solution.py:55
  30.7 0.0 all-gather.5.cloned.1.call-start
  30.7 0.7 all-gather.5.cloned.1.call-update
  31.4 0.0 copy-done.2
  31.4 1.6 convolution_convert_fusion.1
  33.1 3.4 reshape.66
  36.5 0.0 copy-start.3
  36.5 92.3 %all-to-all-done = bf16[64,5,2048]{2,1,0:T(8,128)(2,1)S(1)} async-done(((bf16[64,5,2048]{2,1,0:T(8,128)(2,1)}), bf16[64,5,2048]{2,1,0:T(8,128)(2,1)S(1)}, u32[]{:S(2)}, u32[]{:S(2)}) %all-to-all-start) | async-done | bytes 1310752 | tf_op jit(solution)/shard_map/all_to_all | solution.py:55
  128.7 7.1 %all-to-all-start.2 = ((bf16[64,5,2048]{2,1,0:T(8,128)(2,1)}), bf16[64,5,2048]{2,1,0:T(8,128)(2,1)}, u32[]{:S(2)}, u32[]{:S(2)}) async-start(bf16[64,5,2048]{2,1,0:T(8,128)(2,1)} %reshape.66), calls=%async_computation.2 | async-start | bytes 4194304 | tf_op jit(solution)/shard_map/all_to_all | solution.py:54
  135.8 0.0 all-gather.3.cloned.1.call-start
  135.9 0.7 all-gather.3.cloned.1.call-update
  136.6 97.2 %all-to-all-done.2 = bf16[64,5,2048]{2,1,0:T(8,128)(2,1)} async-done(((bf16[64,5,2048]{2,1,0:T(8,128)(2,1)}), bf16[64,5,2048]{2,1,0:T(8,128)(2,1)}, u32[]{:S(2)}, u32[]{:S(2)}) %all-to-all-start.2) | async-done | bytes 1310752 | tf_op jit(solution)/shard_map/all_to_all | solution.py:54
  233.8 0.0 copy-done.3
  233.8 1.8 stack.2
  235.6 6.4 %all-to-all-start.1 = ((bf16[8,1,256,768]{3,2,1,0:T(8,128)(2,1)}), bf16[8,1,256,768]{3,2,1,0:T(8,128)(2,1)}, u32[]{:S(2)}, u32[]{:S(2)}) async-start(bf16[8,1,256,768]{3,2,1,0:T(8,128)(2,1)} %stack.2), calls=%async_computation.1 | async-start | bytes 6291456 | tf_op jit(solution)/shard_map/all_to_all | solution.py:47
  242.0 0.2 reduce-scatter.2.cloned.1.call-start
  242.2 1.4 reshape.65
  243.7 0.0 copy-start.1
  243.7 2.7 reshape.67
  246.3 40.8 %all-to-all-done.1 = bf16[8,1,256,768]{3,2,1,0:T(8,128)(2,1)} async-done(((bf16[8,1,256,768]{3,2,1,0:T(8,128)(2,1)}), bf16[8,1,256,768]{3,2,1,0:T(8,128)(2,1)}, u32[]{:S(2)}, u32[]{:S(2)}) %all-to-all-start.1) | async-done | bytes 3145760 | tf_op jit(solution)/shard_map/all_to_all | solution.py:47
  287.1 0.0 copy-done.1
  287.1 4.0 fusion.29
  291.1 0.0 all-gather.5.cloned.1.call-done
  291.1 4.0 fusion.2
  295.1 0.0 all-gather.3.cloned.1.call-done
  295.2 0.0 copy-start.6
  295.2 3.1 fusion.6
  298.3 0.0 copy-start.8
  298.3 0.9 copy-done.8
  299.3 0.0 copy-done.6
  299.3 3.7 convolution_convert_fusion
  302.9 0.0 copy-start.5
  302.9 0.0 copy-start.7
  302.9 0.0 reduce-scatter.2.cloned.1.call-update
  302.9 1.2 copy-done.5
  304.1 0.3 copy-done.7
  304.4 0.0 copy-start.4
  304.4 3.6 fusion
  308.1 0.0 copy-done.4
  308.1 2.3 fusion.11
  310.4 2.4 reshape.68
  312.7 105.5 %all_to_all.20 = bf16[64,5,2048]{2,1,0:T(8,128)(2,1)} all-to-all(bf16[64,5,2048]{2,1,0:T(8,128)(2,1)S(1)} %reshape.68), channel_id=1, replica_groups=mesh['dp'=8,'expert'=64] {'expert'}, dimensions={0} | all-to-all | bytes 2621440 | tf_op jit(solution)/shard_map/all_to_all | solution.py:70
  418.2 2.6 reshape.69
  420.8 1.3 convolution_convert_fusion.2
  422.1 0.0 reduce-scatter.2.cloned.1.call-done
  (5 shorter events, 0.1 us)
Async XLA Ops:
  7.2 4.2 copy-start
  13.5 18.0 %copy-start.2 = (bf16[128,2048]{1,0:T(8,128)(2,1)S(1)}, bf16[128,2048]{1,0:T(8,128)(2,1)}, u32[]{:S(2)}) copy-start(bf16[128,2048]{1,0:T(8,128)(2,1)} %param.7) | copy-start | bytes 1572868
  13.5 115.3 %all-to-all-start = ((bf16[64,5,2048]{2,1,0:T(8,128)(2,1)}), bf16[64,5,2048]{2,1,0:T(8,128)(2,1)S(1)}, u32[]{:S(2)}, u32[]{:S(2)}) async-start(bf16[64,5,2048]{2,1,0:T(8,128)(2,1)} %reshape.64), calls=%async_computation | async-start | bytes 4194304 | tf_op jit(solution)/shard_map/all_to_all | solution.py:55
  30.7 260.5 %all-gather.5.cloned.1.call-start = ((), (), s32[]{:S(2)}) async-start(), calls=%async_computation.6 | async-start | bytes 3538944 | tf_op jit(solution)/shard_map/all_gather | solution.py:44
  36.5 197.3 %copy-start.3 = (bf16[1,256,768]{2,1,0:T(8,128)(2,1)S(1)}, bf16[1,256,768]{2,1,0:T(8,128)(2,1)}, u32[]{:S(2)}) copy-start(bf16[1,256,768]{2,1,0:T(8,128)(2,1)} %param.13) | copy-start | bytes 1179652
  128.7 105.1 %all-to-all-start.2 = ((bf16[64,5,2048]{2,1,0:T(8,128)(2,1)}), bf16[64,5,2048]{2,1,0:T(8,128)(2,1)}, u32[]{:S(2)}, u32[]{:S(2)}) async-start(bf16[64,5,2048]{2,1,0:T(8,128)(2,1)} %reshape.66), calls=%async_computation.2 | async-start | bytes 4194304 | tf_op jit(solution)/shard_map/all_to_all | solution.py:54
  135.8 159.3 %all-gather.3.cloned.1.call-start = ((), (), s32[]{:S(2)}) async-start(), calls=%async_computation.5 | async-start | bytes 3538944 | tf_op jit(solution)/shard_map/all_gather | solution.py:45
  235.6 51.5 %all-to-all-start.1 = ((bf16[8,1,256,768]{3,2,1,0:T(8,128)(2,1)}), bf16[8,1,256,768]{3,2,1,0:T(8,128)(2,1)}, u32[]{:S(2)}, u32[]{:S(2)}) async-start(bf16[8,1,256,768]{3,2,1,0:T(8,128)(2,1)} %stack.2), calls=%async_computation.1 | async-start | bytes 6291456 | tf_op jit(solution)/shard_map/all_to_all | solution.py:47
  242.0 180.1 %reduce-scatter.2.cloned.1.call-start = ((), (), s32[]{:S(2)}) async-start(), calls=%async_computation.7 | async-start | bytes 3538944 | tf_op jit(solution)/shard_map/reduce_scatter | solution.py:83
  243.7 43.5 %copy-start.1 = (bf16[320,2048]{1,0:T(8,128)(2,1)S(1)}, bf16[320,2048]{1,0:T(8,128)(2,1)}, u32[]{:S(2)}) copy-start(bf16[320,2048]{1,0:T(8,128)(2,1)} %reshape.65) | copy-start | bytes 3932164
  295.2 4.1 copy-start.6
  298.3 1.0 copy-start.8
  302.9 1.2 copy-start.5
  302.9 1.5 copy-start.7
  304.4 3.7 copy-start.4
Sparse Core Ops, SparseCore 0:
  34.7 86.0 all-gather.4
  139.8 85.7 all-gather.2
  303.1 92.4 reduce-scatter.1
